TPU v7x, 32 devices: a whole 2x2x4 slice. The times are simulated.
32 devices in a mesh: gx: 2 (over core), ga: 4 (over y, x), gz: 4 (over z).
Axes of the slice: x: 2, y: 2, z: 4, core: 2. Of those that a mesh axis runs over, the one named last changes fastest.
Arguments:
- right_side: float32 [32, 64, 512], P('gx', 'ga', 'gz'), may hold values from -15 to 15
- diagonal: float32 [32, 64, 512], P('gx', 'ga', 'gz'), may hold values from 0.25 to 2
- basis_tables: float32 [3, 12, 12], replicated, may hold values from -1.75 to 1.75
- eigenvalues: float32 [3, 12], replicated, may hold values from 0.3 to 3
- coarse_blocks: float32 [2, 4, 4, 2, 64, 64], P('gx', 'ga', 'gz'), may hold values from -1 to 1
- coarse_columns: int32 [2, 4, 4, 2], P('gx', 'ga', 'gz'), may hold values from 0 to 15
Outputs:
- solution: float32 [32, 64, 512], P('gx', 'ga', 'gz')
- residual: float32 [32, 64, 512], P('gx', 'ga', 'gz')
All inputs are finite; a program needn't handle non-finite values.
Results may differ from a plain program's by a relative error of at most 0.0003.
Values sent between devices are 32-bit elements; how exact they have to be, the bound alone decides.
No kernel may reach another device: no remote copies, remote signals or barrier semaphores. Data moves between devices by JAX's collectives and lax.ppermute only.
A program may use at most 64 MiB of HBM per device.

v0:
```python
import jax
import jax.numpy as jnp
from jax import lax
from jax.sharding import PartitionSpec as P

PTS = 8
RIM = 2
WIDE = 12
CYCLES = 2
PRECISE = lax.Precision.HIGHEST


def padded_2(value, sides, width):
    for axis, dim in sides:
        size, length = (lax.axis_size(axis), value.shape[dim])
        up = [(i, (i + 1) % size) for i in range(size - 1)]
        down = [(j, i) for i, j in up]
        last = lax.slice_in_dim(value, length - width, length, axis=dim)
        leading = lax.slice_in_dim(value, 0, width, axis=dim)
        before = lax.ppermute(last, axis, up)
        after = lax.ppermute(leading, axis, down)
        value = jnp.concatenate([before, value, after], axis=dim)
    return value


def operate(field, diagonal):
    padded = padded_2(field, (("gx", 0), ("ga", 1), ("gz", 2)), 1)
    beside = padded[2:, 1:-1, 1:-1] + padded[:-2, 1:-1, 1:-1]
    beside = beside + padded[1:-1, 2:, 1:-1] + padded[1:-1, :-2, 1:-1]
    beside = beside + padded[1:-1, 1:-1, 2:] + padded[1:-1, 1:-1, :-2]
    return (6.0 + diagonal) * field - beside


def forward_table(count, basis):
    row_index = jnp.arange(PTS * count + 2 * RIM, dtype=jnp.int32)
    element = jnp.arange(count, dtype=jnp.int32)
    offset = jnp.arange(WIDE, dtype=jnp.int32)
    select = (
        row_index[:, None, None] == PTS * element[None, :, None] + offset[None, None, :]
    ).astype(jnp.float32)
    table = jnp.einsum("rcj,jm->rcm", select, basis, precision=PRECISE)
    return table.reshape(PTS * count + 2 * RIM, count * WIDE)


def backward_table(count, basis):
    same = jnp.eye(count, dtype=jnp.float32)
    table = jnp.einsum("cd,im->cmdi", same, basis[RIM : RIM + PTS], precision=PRECISE)
    return table.reshape(count * WIDE, count * PTS)


def schwarz_part(field, basis_tables, eigenvalues):
    count_x = field.shape[0] // PTS
    count_y = field.shape[1] // PTS
    count_z = field.shape[2] // PTS
    padded = padded_2(field, (("gx", 0), ("ga", 1), ("gz", 2)), RIM)
    spectral = jnp.einsum(
        "pqr,rc->pqc", padded, forward_table(count_z, basis_tables[2]), precision=PRECISE
    )
    spectral = jnp.einsum(
        "pqc,pa->aqc", spectral, forward_table(count_x, basis_tables[0]), precision=PRECISE
    )
    spectral = jnp.einsum(
        "aqc,qb->abc", spectral, forward_table(count_y, basis_tables[1]), precision=PRECISE
    )
    denominator = (
        jnp.tile(eigenvalues[0], count_x)[:, None, None]
        + jnp.tile(eigenvalues[1], count_y)[None, :, None]
    )
    denominator = denominator + jnp.tile(eigenvalues[2], count_z)[None, None, :]
    spectral = spectral / denominator
    local_part = jnp.einsum(
        "abc,cr->abr", spectral, backward_table(count_z, basis_tables[2]), precision=PRECISE
    )
    local_part = jnp.einsum(
        "abr,ap->pbr", local_part, backward_table(count_x, basis_tables[0]), precision=PRECISE
    )
    local_part = jnp.einsum(
        "pbr,bq->pqr", local_part, backward_table(count_y, basis_tables[1]), precision=PRECISE
    )
    return local_part


def coarse_part(field, blocks, selector):
    count_x = field.shape[0] // PTS
    count_y = field.shape[1] // PTS
    count_z = field.shape[2] // PTS
    cells = count_x * count_y * count_z
    means = jnp.mean(field.reshape(count_x, PTS, count_y, PTS, count_z, PTS), axis=(1, 3, 5))
    restricted = means.reshape(cells)
    terms = jnp.einsum("kpq,p->kq", blocks, restricted, precision=PRECISE)
    buffer = jnp.einsum("kj,kq->jq", selector, terms, precision=PRECISE)
    owned = lax.psum_scatter(buffer, ("ga", "gz"), scatter_dimension=0, tiled=True)
    whole = lax.all_gather(owned, ("ga", "gz"), axis=0, tiled=True)
    picked = jnp.dot(selector, whole, precision=PRECISE)
    coarse = jnp.einsum("kpq,kq->p", blocks, picked, precision=PRECISE)
    coarse = coarse.reshape(count_x, 1, count_y, 1, count_z, 1)
    spread = jnp.broadcast_to(coarse, (count_x, PTS, count_y, PTS, count_z, PTS))
    return spread.reshape(field.shape)


def start_norm(residual):
    return jnp.sqrt(lax.psum(jnp.sum(residual * residual), ("gx", "ga", "gz")))


def body(right_side, diagonal, basis_tables, eigenvalues, coarse_blocks, coarse_columns):
    blocks = coarse_blocks.reshape(coarse_blocks.shape[3:])
    columns = coarse_columns.reshape(coarse_columns.shape[3])
    group = lax.axis_size(("ga", "gz"))
    selector = (columns[:, None] == jnp.arange(group, dtype=jnp.int32)[None, :]).astype(jnp.float32)

    def precondition(field):
        return schwarz_part(field, basis_tables, eigenvalues) + coarse_part(field, blocks, selector)

    solution = jnp.zeros_like(right_side)
    residual = right_side
    for restart in range(CYCLES):
        initial_norm = start_norm(residual)
        first_vector = residual / initial_norm
        first_zed = precondition(first_vector)
        first_image = operate(first_zed, diagonal)
        first_proj, image_square = lax.psum(
            (jnp.sum(first_vector * first_image), jnp.sum(first_image * first_image)),
            ("gx", "ga", "gz"),
        )
        first_ortho = first_image - first_proj * first_vector
        first_len = jnp.sqrt(image_square - first_proj * first_proj)
        second_vector = first_ortho / first_len
        second_zed = precondition(second_vector)
        second_image = operate(second_zed, diagonal)
        upper_proj, lower_proj, second_square = lax.psum(
            (
                jnp.sum(first_vector * second_image),
                jnp.sum(second_vector * second_image),
                jnp.sum(second_image * second_image),
            ),
            ("gx", "ga", "gz"),
        )
        second_len = jnp.sqrt(second_square - upper_proj * upper_proj - lower_proj * lower_proj)
        gram_first = first_proj * first_proj + first_len * first_len
        gram_cross = first_proj * upper_proj + first_len * lower_proj
        gram_second = upper_proj * upper_proj + lower_proj * lower_proj + second_len * second_len
        target_first = initial_norm * first_proj
        target_second = initial_norm * upper_proj
        determinant = gram_first * gram_second - gram_cross * gram_cross
        weight_first = (gram_second * target_first - gram_cross * target_second) / determinant
        weight_second = (gram_first * target_second - gram_cross * target_first) / determinant
        solution = solution + weight_first * first_zed + weight_second * second_zed
        residual = right_side - operate(solution, diagonal)
    return (solution, residual)


def solution(mesh):
    in_specs = (
        P("gx", "ga", "gz"),
        P("gx", "ga", "gz"),
        P(),
        P(),
        P("gx", "ga", "gz", None, None, None),
        P("gx", "ga", "gz", None),
    )
    out_specs = (P("gx", "ga", "gz"), P("gx", "ga", "gz"))
    return jax.shard_map(body, mesh=mesh, in_specs=in_specs, out_specs=out_specs, check_vma=False)
```

profile of v0, /device:TPU:12, one launch (start us, length us, event | category | flops | bytes accessed | tf_op | source)
XLA Modules:
  0.0 856.3 jit_solution(14189468546565872897)
XLA Ops:
  2.2 41.6 %psum.84 = f32[]{:T(128)} all-reduce(f32[]{:T(128)} %multiply_reduce_fusion.11), channel_id=1, replica_groups=mesh['gx'=2,'ga'=4,'gz'=4] {'gx','ga','gz'}, use_global_device_ids=true, to_apply=%region_1.0 | all-reduce | flops 1 | bytes 8 | tf_op jit(solution)/shard_map/psum | solution.py:102
  50.8 37.9 %all-reduce = f32[16,64]{1,0:T(8,128)S(1)} all-reduce(f32[16,64]{1,0:T(8,128)S(1)} %fusion.102), channel_id=2, replica_groups=mesh['gx'=2,'ga'=4,'gz'=4] {'ga','gz'}, use_global_device_ids=true, to_apply=%region_3.0.clone | all-reduce | flops 1024 | bytes 8192
  90.0 38.2 %all-gather = f32[16,1,64]{2,1,0:T(1,128)S(1)} all-gather(f32[1,1,64]{2,1,0:T(1,128)S(1)} %fusion.103), channel_id=1, replica_groups=mesh['gx'=2,'ga'=4,'gz'=4] {'ga','gz'}, dimensions={0}, use_global_device_ids=true | all-gather | bytes 4352 | tf_op jit(solution)/shard_map/all_gather | solution.py:93
  131.2 4.8 collective-permute-start.3
  157.4 5.1 collective-permute-start.8
  164.4 4.5 collective-permute-done.9
  181.8 38.4 %all-reduce.7 = (f32[]{:T(128)}, f32[]{:T(128)}) all-reduce(f32[]{:T(128)} %get-tuple-element.11, f32[]{:T(128)} %get-tuple-element.10), channel_id=1, replica_groups=mesh['gx'=2,'ga'=4,'gz'=4] {'gx','ga','gz'}, use_global_device_ids=true, to_apply=%region_7.0 | all-reduce | flops 2 | bytes 16 | tf_op jit(solution)/shard_map/psum | solution.py:121
  227.4 39.5 %all-reduce.1 = f32[16,64]{1,0:T(8,128)S(1)} all-reduce(f32[16,64]{1,0:T(8,128)S(1)} %fusion.100), channel_id=3, replica_groups=mesh['gx'=2,'ga'=4,'gz'=4] {'ga','gz'}, use_global_device_ids=true, to_apply=%region_9.0.clone | all-reduce | flops 1024 | bytes 8192
  267.5 37.8 %all-gather.1 = f32[16,1,64]{2,1,0:T(1,128)S(1)} all-gather(f32[1,1,64]{2,1,0:T(1,128)S(1)} %fusion.104), channel_id=1, replica_groups=mesh['gx'=2,'ga'=4,'gz'=4] {'ga','gz'}, dimensions={0}, use_global_device_ids=true | all-gather | bytes 4352 | tf_op jit(solution)/shard_map/all_gather | solution.py:93
  307.3 4.8 collective-permute-start.15
  316.4 4.4 collective-permute-start.17
  334.5 5.1 collective-permute-start.20
  341.6 4.5 collective-permute-done.21
  359.0 38.5 %all-reduce.6 = (f32[]{:T(128)}, f32[]{:T(128)}, f32[]{:T(128)}) all-reduce(f32[]{:T(128)} %get-tuple-element.9, f32[]{:T(128)} %get-tuple-element.8, f32[]{:T(128)} %get-tuple-element.7), channel_id=1, replica_groups=mesh['gx'=2,'ga'=4,'gz'=4] {'gx','ga','gz'}, use_global_device_ids=true, to_apply=%region_11.0 | all-reduce | flops 3 | bytes 24 | tf_op jit(solution)/shard_map/psum | solution.py:130
  431.0 38.3 %psum.90 = f32[]{:T(128)} all-reduce(f32[]{:T(128)} %get-tuple-element.23), channel_id=1, replica_groups=mesh['gx'=2,'ga'=4,'gz'=4] {'gx','ga','gz'}, use_global_device_ids=true, to_apply=%region_17.0 | all-reduce | flops 1 | bytes 8 | tf_op jit(solution)/shard_map/psum | solution.py:102
  474.7 39.5 %all-reduce.2 = f32[16,64]{1,0:T(8,128)S(1)} all-reduce(f32[16,64]{1,0:T(8,128)S(1)} %fusion.98), channel_id=4, replica_groups=mesh['gx'=2,'ga'=4,'gz'=4] {'ga','gz'}, use_global_device_ids=true, to_apply=%region_19.0.clone | all-reduce | flops 1024 | bytes 8192
  514.8 37.8 %all-gather.2 = f32[16,1,64]{2,1,0:T(1,128)S(1)} all-gather(f32[1,1,64]{2,1,0:T(1,128)S(1)} %fusion.105), channel_id=1, replica_groups=mesh['gx'=2,'ga'=4,'gz'=4] {'ga','gz'}, dimensions={0}, use_global_device_ids=true | all-gather | bytes 4352 | tf_op jit(solution)/shard_map/all_gather | solution.py:93
  554.6 4.8 collective-permute-start.33
  563.7 4.1 collective-permute-start.35
  581.9 5.1 collective-permute-start.38
  588.9 4.5 collective-permute-done.39
  606.2 38.4 %all-reduce.5 = (f32[]{:T(128)}, f32[]{:T(128)}) all-reduce(f32[]{:T(128)} %get-tuple-element.6, f32[]{:T(128)} %get-tuple-element.5), channel_id=1, replica_groups=mesh['gx'=2,'ga'=4,'gz'=4] {'gx','ga','gz'}, use_global_device_ids=true, to_apply=%region_23.0 | all-reduce | flops 2 | bytes 16 | tf_op jit(solution)/shard_map/psum | solution.py:121
  651.9 39.5 %all-reduce.3 = f32[16,64]{1,0:T(8,128)S(1)} all-reduce(f32[16,64]{1,0:T(8,128)S(1)} %fusion.96), channel_id=5, replica_groups=mesh['gx'=2,'ga'=4,'gz'=4] {'ga','gz'}, use_global_device_ids=true, to_apply=%region_25.0.clone | all-reduce | flops 1024 | bytes 8192
  692.1 37.8 %all-gather.3 = f32[16,1,64]{2,1,0:T(1,128)S(1)} all-gather(f32[1,1,64]{2,1,0:T(1,128)S(1)} %fusion.106), channel_id=1, replica_groups=mesh['gx'=2,'ga'=4,'gz'=4] {'ga','gz'}, dimensions={0}, use_global_device_ids=true | all-gather | bytes 4352 | tf_op jit(solution)/shard_map/all_gather | solution.py:93
  731.8 4.8 collective-permute-start.45
  741.0 4.8 collective-permute-start.47
  759.4 5.1 collective-permute-start.50
  766.5 4.5 collective-permute-done.51
  771.1 4.4 collective-permute-start.52
  779.3 4.1 collective-permute-done.53
  784.3 38.5 %all-reduce.4 = (f32[]{:T(128)}, f32[]{:T(128)}, f32[]{:T(128)}) all-reduce(f32[]{:T(128)} %get-tuple-element.4, f32[]{:T(128)} %get-tuple-element.3, f32[]{:T(128)} %get-tuple-element.2), channel_id=1, replica_groups=mesh['gx'=2,'ga'=4,'gz'=4] {'gx','ga','gz'}, use_global_device_ids=true, to_apply=%region_27.0 | all-reduce | flops 3 | bytes 24 | tf_op jit(solution)/shard_map/psum | solution.py:130
  843.3 4.0 collective-permute-start.58
  (306 shorter events, 210.5 us)
Async XLA Ops:
  45.5 83.7 %collective-permute-start = (f32[2,16,128]{2,1,0:T(8,128)S(1)}, f32[2,16,128]{2,1,0:T(8,128)S(1)}, u32[]{:S(2)}, u32[]{:S(2)}) collective-permute-start(f32[2,16,128]{2,1,0:T(8,128)S(1)} %get-tuple-element.84), channel_id=1, source_target_pairs={{0,16},{1,17},{2,18},{3,19},{4,20},{5,21},{6,22},{7,23},{8,24},{9,... | collective-permute-start | bytes 49160 | tf_op jit(solution)/shard_map/ppermute | solution.py:20
  46.8 82.4 %collective-permute-start.1 = (f32[2,16,128]{2,1,0:T(8,128)S(1)}, f32[2,16,128]{2,1,0:T(8,128)S(1)}, u32[]{:S(2)}, u32[]{:S(2)}) collective-permute-start(f32[2,16,128]{2,1,0:T(8,128)S(1)} %get-tuple-element.85), channel_id=1, source_target_pairs={{16,0},{17,1},{18,2},{19,3},{20,4},{21,5},{22,6},{23,7},{24,8},{25... | collective-permute-start | bytes 49160 | tf_op jit(solution)/shard_map/ppermute | solution.py:21
  138.4 8.3 collective-permute-start.4
  140.3 8.3 collective-permute-start.5
  157.4 7.1 collective-permute-start.8
  169.1 8.1 collective-permute-start.10
  173.1 7.9 collective-permute-start.11
  223.9 81.4 %collective-permute-start.12 = (f32[2,16,128]{2,1,0:T(8,128)S(1)}, f32[2,16,128]{2,1,0:T(8,128)S(1)}, u32[]{:S(2)}, u32[]{:S(2)}) collective-permute-start(f32[2,16,128]{2,1,0:T(8,128)S(1)} %get-tuple-element.80), channel_id=1, source_target_pairs={{0,16},{1,17},{2,18},{3,19},{4,20},{5,21},{6,22},{7,23},{8,24},{9,... | collective-permute-start | bytes 49160 | tf_op jit(solution)/shard_map/ppermute | solution.py:20
  225.3 80.0 %collective-permute-start.13 = (f32[2,16,128]{2,1,0:T(8,128)S(1)}, f32[2,16,128]{2,1,0:T(8,128)S(1)}, u32[]{:S(2)}, u32[]{:S(2)}) collective-permute-start(f32[2,16,128]{2,1,0:T(8,128)S(1)} %get-tuple-element.81), channel_id=1, source_target_pairs={{16,0},{17,1},{18,2},{19,3},{20,4},{21,5},{22,6},{23,7},{24,8},{25... | collective-permute-start | bytes 49160 | tf_op jit(solution)/shard_map/ppermute | solution.py:21
  314.5 8.3 collective-permute-start.16
  316.4 8.4 collective-permute-start.17
  334.5 7.0 collective-permute-start.20
  346.3 8.1 collective-permute-start.22
  350.2 7.9 collective-permute-start.23
  418.3 8.1 collective-permute-start.28
  422.3 7.9 collective-permute-start.29
  471.2 81.5 %collective-permute-start.30 = (f32[2,16,128]{2,1,0:T(8,128)S(1)}, f32[2,16,128]{2,1,0:T(8,128)S(1)}, u32[]{:S(2)}, u32[]{:S(2)}) collective-permute-start(f32[2,16,128]{2,1,0:T(8,128)S(1)} %get-tuple-element.74), channel_id=1, source_target_pairs={{0,16},{1,17},{2,18},{3,19},{4,20},{5,21},{6,22},{7,23},{8,24},{9,... | collective-permute-start | bytes 49160 | tf_op jit(solution)/shard_map/ppermute | solution.py:20
  472.6 80.0 %collective-permute-start.31 = (f32[2,16,128]{2,1,0:T(8,128)S(1)}, f32[2,16,128]{2,1,0:T(8,128)S(1)}, u32[]{:S(2)}, u32[]{:S(2)}) collective-permute-start(f32[2,16,128]{2,1,0:T(8,128)S(1)} %get-tuple-element.75), channel_id=1, source_target_pairs={{16,0},{17,1},{18,2},{19,3},{20,4},{21,5},{22,6},{23,7},{24,8},{25... | collective-permute-start | bytes 49160 | tf_op jit(solution)/shard_map/ppermute | solution.py:21
  561.8 8.3 collective-permute-start.34
  563.7 8.4 collective-permute-start.35
  581.9 7.1 collective-permute-start.38
  593.6 8.1 collective-permute-start.40
  597.5 7.9 collective-permute-start.41
  648.4 81.5 %collective-permute-start.42 = (f32[2,16,128]{2,1,0:T(8,128)S(1)}, f32[2,16,128]{2,1,0:T(8,128)S(1)}, u32[]{:S(2)}, u32[]{:S(2)}) collective-permute-start(f32[2,16,128]{2,1,0:T(8,128)S(1)} %get-tuple-element.70), channel_id=1, source_target_pairs={{0,16},{1,17},{2,18},{3,19},{4,20},{5,21},{6,22},{7,23},{8,24},{9,... | collective-permute-start | bytes 49160 | tf_op jit(solution)/shard_map/ppermute | solution.py:20
  649.9 80.0 %collective-permute-start.43 = (f32[2,16,128]{2,1,0:T(8,128)S(1)}, f32[2,16,128]{2,1,0:T(8,128)S(1)}, u32[]{:S(2)}, u32[]{:S(2)}) collective-permute-start(f32[2,16,128]{2,1,0:T(8,128)S(1)} %get-tuple-element.71), channel_id=1, source_target_pairs={{16,0},{17,1},{18,2},{19,3},{20,4},{21,5},{22,6},{23,7},{24,8},{25... | collective-permute-start | bytes 49160 | tf_op jit(solution)/shard_map/ppermute | solution.py:21
  739.0 8.4 collective-permute-start.46
  741.0 8.6 %collective-permute-start.47 = (f32[20,20,2]{2,1,0:T(8,128)}, f32[20,20,2]{2,1,0:T(8,128)}, u32[]{:S(2)}, u32[]{:S(2)}) collective-permute-start(f32[20,20,2]{2,1,0:T(8,128)} %get-tuple-element.27), channel_id=1, source_target_pairs={{1,0},{2,1},{3,2},{5,4},{6,5},{7,6},{9,8},{10,9},{11,10},{13,12},{... | collective-permute-start | bytes 9608 | tf_op jit(solution)/shard_map/ppermute | solution.py:21
  759.4 7.1 collective-permute-start.50
  771.1 8.1 collective-permute-start.52
  775.5 7.9 collective-permute-start.53
  843.3 8.1 collective-permute-start.58
  847.3 7.9 collective-permute-start.59
  (54 other events, 603.8 us)
where the time goes:
time: 868 us; the launch traced here: 856 us
  blocking collectives  542 us (62%)
  starting transfers between devices  164 us (19%)
  waiting for transfers between devices  79 us (9%)
  between operations  20.5 us (2%)
  local copies, waits for them, and re-layouts  18.6 us (2%)
  matrix products  17.2 us (2%)
  other arithmetic  15.3 us (2%)
    unnamed x4, blocking collectives  156 us
    all_gather x4, blocking collectives, coarse_part(): whole = lax.all_gather(owned, ('ga', 'gz'), axis=0, tiled=True)  152 us
    ppermute x30, starting transfers between devices, padded_2(): after = lax.ppermute(leading, axis, down)  100 us
    psum x2, blocking collectives, start_norm(): return jnp.sqrt(lax.psum(jnp.sum(residual * residual), ('gx', 'ga', 'gz')))  79.9 us
    psum x2, blocking collectives, body(): lax.psum((jnp.sum(first_vector * second_image), jnp.sum(second_vector * s...  76.9 us
    psum x2, blocking collectives, body(): lax.psum((jnp.sum(first_vector * first_image), jnp.sum(first_image * firs...  76.8 us
    ppermute x30, starting transfers between devices, padded_2(): before = lax.ppermute(last, axis, up)  63.7 us
    ppermute x30, waiting for transfers between devices, padded_2(): before = lax.ppermute(last, axis, up)  54 us
  transfers between devices with their start and end apart: 60, of which 35 were waited for; matrix products, arithmetic and copies ran while one was open for 2% of the time, Pallas kernels for 0%

commit v1 on v0

--- a/solution.py
+++ b/solution.py
@@ -90,7 +90,16 @@
     terms = jnp.einsum("kpq,p->kq", blocks, restricted, precision=PRECISE)
     buffer = jnp.einsum("kj,kq->jq", selector, terms, precision=PRECISE)
     owned = lax.psum_scatter(buffer, ("ga", "gz"), scatter_dimension=0, tiled=True)
-    whole = lax.all_gather(owned, ("ga", "gz"), axis=0, tiled=True)
+    ways = lax.axis_size(("ga", "gz"))
+    up_2 = [(d, (d + 1) % ways) for d in range(ways)]
+    down_2 = [(d, (d - 1) % ways) for d in range(ways)]
+    earlier, later = ([owned], [owned])
+    for _ in range(ways // 2):
+        earlier.append(lax.ppermute(earlier[-1], ("ga", "gz"), up_2))
+    for _ in range((ways - 1) // 2):
+        later.append(lax.ppermute(later[-1], ("ga", "gz"), down_2))
+    line = jnp.concatenate([*earlier[::-1], *later[1:]], axis=0)
+    whole = jnp.roll(line, (lax.axis_index(("ga", "gz")) - ways // 2) * owned.shape[0], axis=0)
     picked = jnp.dot(selector, whole, precision=PRECISE)
     coarse = jnp.einsum("kpq,kq->p", blocks, picked, precision=PRECISE)
     coarse = coarse.reshape(count_x, 1, count_y, 1, count_z, 1)

time: 868 us -> 945 us (1.089)
  starting transfers between devices: 164 us -> 322 us
  blocking collectives: 542 us -> 391 us
  waiting for transfers between devices: 79 us -> 148 us
    all_gather x4 -> x0, blocking collectives: 152 us -> none  [coarse_part(): whole = lax.all_gather(owned, ('ga', 'gz'), axis=0, tiled=True)]
    ppermute x0 -> x60, starting transfers between devices: none -> 146 us  [the longest x28 146 us: coarse_part(): later.append(lax.ppermute(later[-1], ('ga', 'gz'), down_2))]
    ppermute x0 -> x60, waiting for transfers between devices: none -> 68 us  [the longest x32 67.6 us: coarse_part(): earlier.append(lax.ppermute(earlier[-1], ('ga', 'gz'), up_2))]
    ppermute x30, starting transfers between devices: 100 us -> 112 us  [padded_2(): after = lax.ppermute(leading, axis, down)]
  transfers between devices with their start and end apart: 60 -> 120, of which waited for: 35 -> 68; matrix products, arithmetic and copies ran while one was open for 2% -> 1% of each run, Pallas kernels for 0% -> 0%
where the time goes in v1:
time: 945 us; the launch traced here: 934 us
  blocking collectives  391 us (41%)
  starting transfers between devices  322 us (34%)
  waiting for transfers between devices  148 us (16%)
  between operations  21.2 us (2%)
  local copies, waits for them, and re-layouts  19.3 us (2%)
  matrix products  17.2 us (2%)
  other arithmetic  16.1 us (2%)
    unnamed x4, blocking collectives  156 us
    ppermute x28, starting transfers between devices, coarse_part(): later.append(lax.ppermute(later[-1], ('ga', 'gz'), down_2))  146 us
    ppermute x30, starting transfers between devices, padded_2(): after = lax.ppermute(leading, axis, down)  112 us
    psum x2, blocking collectives, start_norm(): return jnp.sqrt(lax.psum(jnp.sum(residual * residual), ('gx', 'ga', 'gz')))  80.1 us
    psum x2, blocking collectives, body(): lax.psum((jnp.sum(first_vector * first_image), jnp.sum(first_image * firs...  77.2 us
    psum x2, blocking collectives, body(): lax.psum((jnp.sum(first_vector * second_image), jnp.sum(second_vector * s...  77 us
    ppermute x32, waiting for transfers between devices, coarse_part(): earlier.append(lax.ppermute(earlier[-1], ('ga', 'gz'), up_2))  67.6 us
    ppermute x30, starting transfers between devices, padded_2(): before = lax.ppermute(last, axis, up)  63.7 us
  transfers between devices with their start and end apart: 120, of which 68 were waited for; matrix products, arithmetic and copies ran while one was open for 1% of the time, Pallas kernels for 0%

profile of v1, /device:TPU:12, one launch (start us, length us, event | category | flops | bytes accessed | tf_op | source)
XLA Modules:
  0.0 934.2 jit_solution(6014687145433446364)
XLA Ops:
  2.2 41.6 %psum.84 = f32[]{:T(128)} all-reduce(f32[]{:T(128)} %multiply_reduce_fusion.11), channel_id=1, replica_groups=mesh['gx'=2,'ga'=4,'gz'=4] {'gx','ga','gz'}, use_global_device_ids=true, to_apply=%region_1.0 | all-reduce | flops 1 | bytes 8 | tf_op jit(solution)/shard_map/psum | solution.py:111
  47.4 37.9 %all-reduce = f32[16,64]{1,0:T(8,128)S(1)} all-reduce(f32[16,64]{1,0:T(8,128)S(1)} %fusion.114), channel_id=2, replica_groups=mesh['gx'=2,'ga'=4,'gz'=4] {'ga','gz'}, use_global_device_ids=true, to_apply=%region_3.0.clone | all-reduce | flops 1024 | bytes 8192
  108.0 5.6 collective-permute-start.17
  115.2 5.6 collective-permute-start.18
  122.3 5.7 collective-permute-start.19
  130.1 5.7 collective-permute-start.20
  137.0 6.7 collective-permute-done.13
  154.8 6.9 collective-permute-start.5
  199.3 38.9 %all-reduce.7 = (f32[]{:T(128)}, f32[]{:T(128)}) all-reduce(f32[]{:T(128)} %get-tuple-element.12, f32[]{:T(128)} %get-tuple-element.11), channel_id=1, replica_groups=mesh['gx'=2,'ga'=4,'gz'=4] {'gx','ga','gz'}, use_global_device_ids=true, to_apply=%region_7.9 | all-reduce | flops 2 | bytes 16 | tf_op jit(solution)/shard_map/psum | solution.py:130
  245.4 39.5 %all-reduce.1 = f32[16,64]{1,0:T(8,128)S(1)} all-reduce(f32[16,64]{1,0:T(8,128)S(1)} %fusion.113), channel_id=3, replica_groups=mesh['gx'=2,'ga'=4,'gz'=4] {'ga','gz'}, use_global_device_ids=true, to_apply=%region_9.11.clone | all-reduce | flops 1024 | bytes 8192
  296.8 5.6 collective-permute-start.43
  303.9 5.6 collective-permute-start.44
  311.1 5.6 collective-permute-start.45
  318.2 5.6 collective-permute-start.46
  325.4 5.6 collective-permute-start.47
  332.5 7.1 collective-permute-done.40
  350.7 6.9 collective-permute-start.32
  396.3 38.5 %all-reduce.6 = (f32[]{:T(128)}, f32[]{:T(128)}, f32[]{:T(128)}) all-reduce(f32[]{:T(128)} %get-tuple-element.10, f32[]{:T(128)} %get-tuple-element.9, f32[]{:T(128)} %get-tuple-element.8), channel_id=1, replica_groups=mesh['gx'=2,'ga'=4,'gz'=4] {'gx','ga','gz'}, use_global_device_ids=true, to_apply=%region_11.13 | all-reduce | flops 3 | bytes 24 | tf_op jit(solution)/shard_map/psum | solution.py:139
  468.4 38.5 %psum.90 = f32[]{:T(128)} all-reduce(f32[]{:T(128)} %get-tuple-element.24), channel_id=1, replica_groups=mesh['gx'=2,'ga'=4,'gz'=4] {'gx','ga','gz'}, use_global_device_ids=true, to_apply=%region_17.19 | all-reduce | flops 1 | bytes 8 | tf_op jit(solution)/shard_map/psum | solution.py:111
  512.3 39.5 %all-reduce.2 = f32[16,64]{1,0:T(8,128)S(1)} all-reduce(f32[16,64]{1,0:T(8,128)S(1)} %fusion.112), channel_id=4, replica_groups=mesh['gx'=2,'ga'=4,'gz'=4] {'ga','gz'}, use_global_device_ids=true, to_apply=%region_19.21.clone | all-reduce | flops 1024 | bytes 8192
  599.4 7.1 collective-permute-done.73
  619.0 6.9 collective-permute-start.65
  664.4 38.4 %all-reduce.5 = (f32[]{:T(128)}, f32[]{:T(128)}) all-reduce(f32[]{:T(128)} %get-tuple-element.7, f32[]{:T(128)} %get-tuple-element.6), channel_id=1, replica_groups=mesh['gx'=2,'ga'=4,'gz'=4] {'gx','ga','gz'}, use_global_device_ids=true, to_apply=%region_23.25 | all-reduce | flops 2 | bytes 16 | tf_op jit(solution)/shard_map/psum | solution.py:130
  710.2 39.5 %all-reduce.3 = f32[16,64]{1,0:T(8,128)S(1)} all-reduce(f32[16,64]{1,0:T(8,128)S(1)} %fusion.111), channel_id=5, replica_groups=mesh['gx'=2,'ga'=4,'gz'=4] {'ga','gz'}, use_global_device_ids=true, to_apply=%region_25.27.clone | all-reduce | flops 1024 | bytes 8192
  761.5 5.8 collective-permute-start.103
  768.7 5.6 collective-permute-start.104
  775.8 5.6 collective-permute-start.105
  782.9 5.6 collective-permute-start.106
  790.1 5.6 collective-permute-start.107
  797.2 7.1 collective-permute-done.100
  815.5 7.6 collective-permute-start.92
  861.8 38.5 %all-reduce.4 = (f32[]{:T(128)}, f32[]{:T(128)}, f32[]{:T(128)}) all-reduce(f32[]{:T(128)} %get-tuple-element.5, f32[]{:T(128)} %get-tuple-element.4, f32[]{:T(128)} %get-tuple-element.3), channel_id=1, replica_groups=mesh['gx'=2,'ga'=4,'gz'=4] {'gx','ga','gz'}, use_global_device_ids=true, to_apply=%region_27.29 | all-reduce | flops 3 | bytes 24 | tf_op jit(solution)/shard_map/psum | solution.py:139
  (408 shorter events, 386.9 us)
Async XLA Ops:
  89.7 54.1 %collective-permute-start = (f32[2,16,128]{2,1,0:T(8,128)S(1)}, f32[2,16,128]{2,1,0:T(8,128)S(1)}, u32[]{:S(2)}, u32[]{:S(2)}) collective-permute-start(f32[2,16,128]{2,1,0:T(8,128)S(1)} %get-tuple-element.85), channel_id=1, source_target_pairs={{0,16},{1,17},{2,18},{3,19},{4,20},{5,21},{6,22},{7,23},{8,24},{9,... | collective-permute-start | bytes 49160 | tf_op jit(solution)/shard_map/ppermute | solution.py:20
  90.9 52.8 %collective-permute-start.1 = (f32[2,16,128]{2,1,0:T(8,128)S(1)}, f32[2,16,128]{2,1,0:T(8,128)S(1)}, u32[]{:S(2)}, u32[]{:S(2)}) collective-permute-start(f32[2,16,128]{2,1,0:T(8,128)S(1)} %get-tuple-element.86), channel_id=1, source_target_pairs={{16,0},{17,1},{18,2},{19,3},{20,4},{21,5},{22,6},{23,7},{24,8},{25... | collective-permute-start | bytes 49160 | tf_op jit(solution)/shard_map/ppermute | solution.py:21
  108.0 7.1 collective-permute-start.17
  115.2 7.1 collective-permute-start.10
  115.2 7.2 collective-permute-start.18
  122.3 7.7 collective-permute-start.19
  152.9 11.3 %collective-permute-start.4 = (f32[20,20,2]{2,1,0:T(8,128)}, f32[20,20,2]{2,1,0:T(8,128)S(1)}, u32[]{:S(2)}, u32[]{:S(2)}) collective-permute-start(f32[20,20,2]{2,1,0:T(8,128)} %get-tuple-element.33), channel_id=1, source_target_pairs={{0,1},{1,2},{2,3},{4,5},{5,6},{6,7},{8,9},{9,10},{10,11},{12,13},{... | collective-permute-start | bytes 9608 | tf_op jit(solution)/shard_map/ppermute | solution.py:20
  154.8 10.9 %collective-permute-start.5 = (f32[20,20,2]{2,1,0:T(8,128)}, f32[20,20,2]{2,1,0:T(8,128)S(1)}, u32[]{:S(2)}, u32[]{:S(2)}) collective-permute-start(f32[20,20,2]{2,1,0:T(8,128)} %get-tuple-element.34), channel_id=1, source_target_pairs={{1,0},{2,1},{3,2},{5,4},{6,5},{7,6},{9,8},{10,9},{11,10},{13,12},{... | collective-permute-start | bytes 9608 | tf_op jit(solution)/shard_map/ppermute | solution.py:21
  186.3 8.1 collective-permute-start.25
  190.6 7.9 collective-permute-start.26
  241.9 97.7 %collective-permute-start.27 = (f32[2,16,128]{2,1,0:T(8,128)S(1)}, f32[2,16,128]{2,1,0:T(8,128)S(1)}, u32[]{:S(2)}, u32[]{:S(2)}) collective-permute-start(f32[2,16,128]{2,1,0:T(8,128)S(1)} %get-tuple-element.81), channel_id=1, source_target_pairs={{0,16},{1,17},{2,18},{3,19},{4,20},{5,21},{6,22},{7,23},{8,24},{9,... | collective-permute-start | bytes 49160 | tf_op jit(solution)/shard_map/ppermute | solution.py:20
  243.4 96.3 %collective-permute-start.28 = (f32[2,16,128]{2,1,0:T(8,128)S(1)}, f32[2,16,128]{2,1,0:T(8,128)S(1)}, u32[]{:S(2)}, u32[]{:S(2)}) collective-permute-start(f32[2,16,128]{2,1,0:T(8,128)S(1)} %get-tuple-element.82), channel_id=1, source_target_pairs={{16,0},{17,1},{18,2},{19,3},{20,4},{21,5},{22,6},{23,7},{24,8},{25... | collective-permute-start | bytes 49160 | tf_op jit(solution)/shard_map/ppermute | solution.py:21
  348.8 11.3 %collective-permute-start.31 = (f32[20,20,2]{2,1,0:T(8,128)}, f32[20,20,2]{2,1,0:T(8,128)S(1)}, u32[]{:S(2)}, u32[]{:S(2)}) collective-permute-start(f32[20,20,2]{2,1,0:T(8,128)} %get-tuple-element.31), channel_id=1, source_target_pairs={{0,1},{1,2},{2,3},{4,5},{5,6},{6,7},{8,9},{9,10},{10,11},{12,13},{... | collective-permute-start | bytes 9608 | tf_op jit(solution)/shard_map/ppermute | solution.py:20
  350.7 11.3 %collective-permute-start.32 = (f32[20,20,2]{2,1,0:T(8,128)}, f32[20,20,2]{2,1,0:T(8,128)}, u32[]{:S(2)}, u32[]{:S(2)}) collective-permute-start(f32[20,20,2]{2,1,0:T(8,128)} %get-tuple-element.32), channel_id=1, source_target_pairs={{1,0},{2,1},{3,2},{5,4},{6,5},{7,6},{9,8},{10,9},{11,10},{13,12},{... | collective-permute-start | bytes 9608 | tf_op jit(solution)/shard_map/ppermute | solution.py:21
  383.1 8.1 collective-permute-start.52
  387.5 7.9 collective-permute-start.53
  455.7 8.1 collective-permute-start.58
  459.7 7.9 collective-permute-start.59
  508.8 97.7 %collective-permute-start.60 = (f32[2,16,128]{2,1,0:T(8,128)S(1)}, f32[2,16,128]{2,1,0:T(8,128)S(1)}, u32[]{:S(2)}, u32[]{:S(2)}) collective-permute-start(f32[2,16,128]{2,1,0:T(8,128)S(1)} %get-tuple-element.75), channel_id=1, source_target_pairs={{0,16},{1,17},{2,18},{3,19},{4,20},{5,21},{6,22},{7,23},{8,24},{9,... | collective-permute-start | bytes 49160 | tf_op jit(solution)/shard_map/ppermute | solution.py:20
  510.2 96.3 %collective-permute-start.61 = (f32[2,16,128]{2,1,0:T(8,128)S(1)}, f32[2,16,128]{2,1,0:T(8,128)S(1)}, u32[]{:S(2)}, u32[]{:S(2)}) collective-permute-start(f32[2,16,128]{2,1,0:T(8,128)S(1)} %get-tuple-element.76), channel_id=1, source_target_pairs={{16,0},{17,1},{18,2},{19,3},{20,4},{21,5},{22,6},{23,7},{24,8},{25... | collective-permute-start | bytes 49160 | tf_op jit(solution)/shard_map/ppermute | solution.py:21
  617.0 11.3 %collective-permute-start.64 = (f32[20,20,2]{2,1,0:T(8,128)}, f32[20,20,2]{2,1,0:T(8,128)S(1)}, u32[]{:S(2)}, u32[]{:S(2)}) collective-permute-start(f32[20,20,2]{2,1,0:T(8,128)} %get-tuple-element.29), channel_id=1, source_target_pairs={{0,1},{1,2},{2,3},{4,5},{5,6},{6,7},{8,9},{9,10},{10,11},{12,13},{... | collective-permute-start | bytes 9608 | tf_op jit(solution)/shard_map/ppermute | solution.py:20
  619.0 11.3 %collective-permute-start.65 = (f32[20,20,2]{2,1,0:T(8,128)}, f32[20,20,2]{2,1,0:T(8,128)}, u32[]{:S(2)}, u32[]{:S(2)}) collective-permute-start(f32[20,20,2]{2,1,0:T(8,128)} %get-tuple-element.30), channel_id=1, source_target_pairs={{1,0},{2,1},{3,2},{5,4},{6,5},{7,6},{9,8},{10,9},{11,10},{13,12},{... | collective-permute-start | bytes 9608 | tf_op jit(solution)/shard_map/ppermute | solution.py:21
  651.3 8.1 collective-permute-start.85
  655.7 7.9 collective-permute-start.86
  706.7 97.7 %collective-permute-start.87 = (f32[2,16,128]{2,1,0:T(8,128)S(1)}, f32[2,16,128]{2,1,0:T(8,128)S(1)}, u32[]{:S(2)}, u32[]{:S(2)}) collective-permute-start(f32[2,16,128]{2,1,0:T(8,128)S(1)} %get-tuple-element.71), channel_id=1, source_target_pairs={{0,16},{1,17},{2,18},{3,19},{4,20},{5,21},{6,22},{7,23},{8,24},{9,... | collective-permute-start | bytes 49160 | tf_op jit(solution)/shard_map/ppermute | solution.py:20
  708.1 96.3 %collective-permute-start.88 = (f32[2,16,128]{2,1,0:T(8,128)S(1)}, f32[2,16,128]{2,1,0:T(8,128)S(1)}, u32[]{:S(2)}, u32[]{:S(2)}) collective-permute-start(f32[2,16,128]{2,1,0:T(8,128)S(1)} %get-tuple-element.72), channel_id=1, source_target_pairs={{16,0},{17,1},{18,2},{19,3},{20,4},{21,5},{22,6},{23,7},{24,8},{25... | collective-permute-start | bytes 49160 | tf_op jit(solution)/shard_map/ppermute | solution.py:21
  813.5 11.4 %collective-permute-start.91 = (f32[20,20,2]{2,1,0:T(8,128)}, f32[20,20,2]{2,1,0:T(8,128)}, u32[]{:S(2)}, u32[]{:S(2)}) collective-permute-start(f32[20,20,2]{2,1,0:T(8,128)} %get-tuple-element.27), channel_id=1, source_target_pairs={{0,1},{1,2},{2,3},{4,5},{5,6},{6,7},{8,9},{9,10},{10,11},{12,13},{... | collective-permute-start | bytes 9608 | tf_op jit(solution)/shard_map/ppermute | solution.py:20
  815.5 11.6 %collective-permute-start.92 = (f32[20,20,2]{2,1,0:T(8,128)}, f32[20,20,2]{2,1,0:T(8,128)}, u32[]{:S(2)}, u32[]{:S(2)}) collective-permute-start(f32[20,20,2]{2,1,0:T(8,128)} %get-tuple-element.28), channel_id=1, source_target_pairs={{1,0},{2,1},{3,2},{5,4},{6,5},{7,6},{9,8},{10,9},{11,10},{13,12},{... | collective-permute-start | bytes 9608 | tf_op jit(solution)/shard_map/ppermute | solution.py:21
  848.6 8.1 collective-permute-start.112
  853.0 7.9 collective-permute-start.113
  921.2 8.1 collective-permute-start.118
  925.2 7.9 collective-permute-start.119
  (105 other events, 1396.6 us)
